TPU v7x, 128 devices: a whole 4x4x4 slice. The times are simulated.
128 devices in a mesh: rep: 16 (over z_lo, x, core), shard: 8 (over z_hi, y).
Axes of the slice: x: 4, y: 4, z: 4 (z_hi: 2, z_lo: 2; z = z_hi * 2 + z_lo), core: 2. Of those that a mesh axis runs over, the one named last changes fastest.
Arguments:
- grad_embed: bfloat16 [16, 8, 4096, 768], P('rep', 'shard'), may hold values from -800 to 800
- grad_proj: bfloat16 [16, 8, 768, 768], P('rep', 'shard'), may hold values from -800 to 800
- grad_norms: bfloat16 [16, 8, 4, 768], P('rep', 'shard'), may hold values from -800 to 800
- embed_master: float32 [4096, 768], P('shard'), may hold values from -0.75 to 0.75
- embed_first: float32 [4096, 768], P('shard'), may hold values from -6 to 6
- embed_second: float32 [4096, 768], P('shard'), may hold values from 0.01 to 4
- proj_master: float32 [768, 768], P('shard'), may hold values from -0.21875 to 0.21875
- proj_first: float32 [768, 768], P('shard'), may hold values from -6 to 6
- proj_second: float32 [768, 768], P('shard'), may hold values from 0.01 to 4
- norm_master: float32 [4, 768], P(None, 'shard'), may hold values from -6 to 6
- norm_first: float32 [4, 768], P(None, 'shard'), may hold values from -6 to 6
- norm_second: float32 [4, 768], P(None, 'shard'), may hold values from 0.01 to 4
Outputs:
- embed_master_new: float32 [4096, 768], P('shard')
- embed_first_new: float32 [4096, 768], P('shard')
- embed_second_new: float32 [4096, 768], P('shard')
- embed_weights: bfloat16 [4096, 768], replicated
- proj_master_new: float32 [768, 768], P('shard')
- proj_first_new: float32 [768, 768], P('shard')
- proj_second_new: float32 [768, 768], P('shard')
- proj_weights: bfloat16 [768, 768], replicated
- norm_master_new: float32 [4, 768], P(None, 'shard')
- norm_first_new: float32 [4, 768], P(None, 'shard')
- norm_second_new: float32 [4, 768], P(None, 'shard')
- norm_weights: bfloat16 [4, 768], replicated
All inputs are finite; a program needn't handle non-finite values.
Results may differ from a plain program's by a relative error of at most 0.0004.
Values may be sent and summed in bfloat16 or wider, within the bound.
No kernel may reach another device: no remote copies, remote signals or barrier semaphores. Data moves between devices by JAX's collectives and lax.ppermute only.
A program may use at most 128 MiB of HBM per device.

v0:
```python
import jax
import jax.numpy as jnp
from jax import lax
from jax.sharding import PartitionSpec as P

beta_one = 0.9
beta_two = 0.95
adam_step = 10.0
adam_eps = 1e-08
learning_rate = 0.002
clip_rms = 1.0

ALL = ("shard", "rep_hi", "core")
HALF = ("shard", "rep_hi")
REP = ("rep_hi", "core")


def adamw(gradient, master, first, second, weight_decay):
    corr_one = 1.0 - beta_one**adam_step
    corr_two = 1.0 - beta_two**adam_step
    first_new = beta_one * first + (1.0 - beta_one) * gradient
    second_new = beta_two * second + (1.0 - beta_two) * gradient * gradient
    direction = (
        first_new / corr_one / (jnp.sqrt(second_new / corr_two) + adam_eps) + weight_decay * master
    )
    master_new = master - learning_rate * direction
    return (master_new, first_new, second_new, master_new.astype(jnp.bfloat16))


def gather_all(piece, axis):
    count = lax.psum(1, axis)
    return lax.all_to_all(
        jnp.broadcast_to(piece[None], (count,) + piece.shape), axis, 0, 0, tiled=True
    )


def shards(
    grad_embed,
    grad_proj,
    grad_norms,
    embed_master,
    embed_first,
    embed_second,
    proj_master,
    proj_first,
    proj_second,
    norm_master,
    norm_first,
    norm_second,
):
    n_rep = lax.psum(1, ("rep_hi", "core"))
    n_shard = lax.psum(1, "shard")
    n_all = n_rep * n_shard
    rep_index = lax.axis_index(("rep_hi", "core"))
    core = lax.axis_index("core")

    embed_rows, width = grad_embed.shape[2:]
    proj_rows = grad_proj.shape[2]
    norm_rows, norm_cols = grad_norms.shape[2:]
    e_rows = embed_rows // n_all
    p_rows = proj_rows // n_all
    n_vals = norm_rows * norm_cols // n_all
    block_norm = norm_cols // n_shard
    rows = e_rows + p_rows + 2
    entry_count = float(embed_rows * width + proj_rows * width + norm_rows * norm_cols)

    embed_send = grad_embed[0, 0].reshape(n_all, e_rows, width)
    proj_send = grad_proj[0, 0].reshape(n_all, p_rows, width)
    norm_send = (
        grad_norms[0, 0]
        .reshape(norm_rows, n_shard, block_norm)
        .transpose(1, 0, 2)
        .reshape(n_all, 1, n_vals)
    )
    norm_send = jnp.pad(norm_send, ((0, 0), (0, 1), (0, width - n_vals)))
    send = jnp.concatenate([embed_send, proj_send, norm_send], axis=1)

    received = lax.all_to_all(send, ALL, 0, 0, tiled=True)
    reduced = jnp.sum(received.astype(jnp.float32), axis=0)

    block = gather_all(reduced, REP)
    embed_sum = block[:, :e_rows].reshape(n_rep * e_rows, width)
    proj_sum = block[:, e_rows : e_rows + p_rows].reshape(n_rep * p_rows, width)
    norm_sum = block[:, e_rows + p_rows, :n_vals].reshape(norm_rows, block_norm)
    partial = jnp.sum(block * block)
    squares = jnp.sum(gather_all(partial.reshape(1), "shard"))
    rms_value = jnp.sqrt(squares / entry_count)
    clip_factor = jnp.minimum(jnp.float32(1.0), clip_rms / (rms_value + 1e-06))

    embed_out = adamw(clip_factor * embed_sum, embed_master, embed_first, embed_second, 0.01)
    proj_out = adamw(clip_factor * proj_sum, proj_master, proj_first, proj_second, 0.01)
    norm_out = adamw(clip_factor * norm_sum, norm_master, norm_first, norm_second, 0.0)
    flat_weights = norm_out[3].reshape(-1)
    w_piece = jnp.concatenate(
        [
            lax.dynamic_slice_in_dim(embed_out[3], rep_index * e_rows, e_rows),
            lax.dynamic_slice_in_dim(proj_out[3], rep_index * p_rows, p_rows),
            jnp.pad(
                lax.dynamic_slice(flat_weights, (rep_index * n_vals,), (n_vals,)).reshape(1, n_vals),
                ((0, 1), (0, width - n_vals)),
            ),
        ],
        axis=0,
    )
    w_mine = gather_all(w_piece, HALF)
    w_other = lax.ppermute(w_mine, "core", [(0, 1), (1, 0)])

    def interleave(lo, hi):
        mine, other = w_mine[:, lo:hi], w_other[:, lo:hi]
        pair = [jnp.where(core == 0, mine, other), jnp.where(core == 0, other, mine)]
        return jnp.stack(pair, axis=1).reshape((n_all, hi - lo) + w_piece.shape[1:])

    embed_weights = interleave(0, e_rows).reshape(embed_rows, width)
    proj_weights = interleave(e_rows, e_rows + p_rows).reshape(proj_rows, width)
    norm_weights = (
        interleave(e_rows + p_rows, e_rows + p_rows + 1)[:, 0, :n_vals]
        .reshape(n_shard, norm_rows, block_norm)
        .transpose(1, 0, 2)
        .reshape(norm_rows, norm_cols)
    )
    return (
        embed_out[0],
        embed_out[1],
        embed_out[2],
        embed_weights,
        proj_out[0],
        proj_out[1],
        proj_out[2],
        proj_weights,
        norm_out[0],
        norm_out[1],
        norm_out[2],
        norm_weights,
    )


def solution(mesh):
    n_rep, n_shard = mesh.devices.shape
    fine = jax.sharding.Mesh(
        mesh.devices.reshape(n_rep // 2, 2, n_shard), ("rep_hi", "core", "shard")
    )
    rep = ("rep_hi", "core")
    return jax.shard_map(
        shards,
        mesh=fine,
        in_specs=(
            P(rep, "shard", None, None),
            P(rep, "shard", None, None),
            P(rep, "shard", None, None),
            P("shard", None),
            P("shard", None),
            P("shard", None),
            P("shard", None),
            P("shard", None),
            P("shard", None),
            P(None, "shard"),
            P(None, "shard"),
            P(None, "shard"),
        ),
        out_specs=(
            P("shard", None),
            P("shard", None),
            P("shard", None),
            P(),
            P("shard", None),
            P("shard", None),
            P("shard", None),
            P(),
            P(None, "shard"),
            P(None, "shard"),
            P(None, "shard"),
            P(),
        ),
        check_vma=False,
    )
```

profile of v0, /device:TPU:1, one launch (start us, length us, event | category | flops | bytes accessed | tf_op | source)
XLA Modules:
  0.0 240.2 jit_solution(14469530298752480395)
XLA Ops:
  0.7 2.2 reshape_squeeze.14
  2.9 0.1 reshape_squeeze.15
  3.0 0.1 reshape.60
  3.1 3.8 %fusion.1 = bf16[128,40,768]{2,1,0:T(8,128)(2,1)S(1)} fusion(bf16[128,1,24]{2,1,0:T(2,128)(2,1)S(1)} %reshape.60, bf16[128,6,768]{2,1,0:T(8,128)(2,1)S(1)} %reshape_squeeze.14, bf16[128,32,768]{2,1,0:T(8,128)(2,1)} %bitcast.36), kind=kLoop, calls=%fused_computation.3 | loop fusion | flops 31457280 | bytes 15341568 | tf_op jit(solution)/shard_map/concatenate | solution.py:76
  6.9 103.4 %all_to_all.21 = bf16[128,40,768]{2,1,0:T(8,128)(2,1)S(1)} all-to-all(bf16[128,40,768]{2,1,0:T(8,128)(2,1)S(1)} %fusion.1), channel_id=1, replica_groups=mesh['rep_hi'=8,'core'=2,'shard'=8] {'shard','rep_hi','core'}, dimensions={0} | all-to-all | bytes 15728640 | tf_op jit(solution)/shard_map/all_to_all | solution.py:78
  110.3 1.1 convert_reduce_fusion
  111.4 1.4 broadcast_in_dim.6
  112.8 4.6 %all-to-all-start.1 = ((f32[16,40,768]{2,1,0:T(8,128)}), f32[16,40,768]{2,1,0:T(8,128)S(1)}, u32[]{:S(2)}, u32[]{:S(2)}) async-start(f32[16,40,768]{2,1,0:T(8,128)} %broadcast_in_dim.6), calls=%async_computation.1 | async-start | bytes 3932160 | tf_op jit(solution)/shard_map/all_to_all | solution.py:32
  117.4 0.0 copy-start.10
  117.4 0.0 copy-start.11
  117.5 0.0 copy-start.5
  117.5 0.0 copy-start.6
  117.5 0.0 copy-start.7
  117.5 25.7 %all-to-all-done.1 = f32[16,40,768]{2,1,0:T(8,128)S(1)} async-done(((f32[16,40,768]{2,1,0:T(8,128)}), f32[16,40,768]{2,1,0:T(8,128)S(1)}, u32[]{:S(2)}, u32[]{:S(2)}) %all-to-all-start.1) | async-done | bytes 1966112 | tf_op jit(solution)/shard_map/all_to_all | solution.py:32
  143.2 1.1 multiply_reduce_fusion
  144.3 0.6 broadcast_in_dim.7
  145.0 10.6 %all_to_all.22 = f32[8,1,1]{2,1,0:T(1,128)S(1)} all-to-all(f32[8,1,1]{2,1,0:T(1,128)S(1)} %broadcast_in_dim.7), channel_id=1, replica_groups=mesh['rep_hi'=8,'core'=2,'shard'=8] {'shard'}, dimensions={0} | all-to-all | bytes 64 | tf_op jit(solution)/shard_map/all_to_all | solution.py:32
  155.5 0.6 reduce_sum.29
  157.0 0.1 mul.199
  157.1 0.0 copy-done.9
  157.1 0.6 fusion.10
  157.7 0.1 reshape.56
  157.8 0.0 copy-start.3
  157.8 1.0 multiply_subtract_fusion.1
  158.9 0.0 copy-start.1
  158.9 0.0 copy-start.2
  158.9 0.2 slice_multiply_fusion
  159.1 0.5 copy-done.4
  159.6 0.9 copy-done.1
  160.5 0.5 copy-done.2
  161.0 2.8 %multiply_subtract_fusion = (f32[512,768]{1,0:T(8,128)S(1)}, f32[512,768]{1,0:T(8,128)}, f32[512,768]{1,0:T(8,128)}) fusion(f32[512,768]{1,0:T(8,128)S(1)} %copy-done.1, f32[16,32,768]{2,1,0:T(8,128)S(1)} %slice_multiply_fusion, f32[512,768]{1,0:T(8,128)S(1)} %copy-done.2, f32[512,768]{1,0:T(8,128)S(1)} %copy-done.3), kind=kLoop, calls=%fused_computation.14 | loop fusion | flops 5898240 | bytes 11010048 | tf_op jit(solution)/shard_map/sub | solution.py:26
  163.8 0.1 dynamic-slice_bitcast_fusion
  163.9 0.3 broadcast_in_dim.8
  164.2 0.8 copy-done
  164.9 53.4 %all_to_all.23 = bf16[64,40,768]{2,1,0:T(8,128)(2,1)} all-to-all(bf16[64,40,768]{2,1,0:T(8,128)(2,1)S(1)} %broadcast_in_dim.8), channel_id=1, replica_groups=mesh['rep_hi'=8,'core'=2,'shard'=8] {'shard','rep_hi'}, dimensions={0} | all-to-all | bytes 7864320 | tf_op jit(solution)/shard_map/all_to_all | solution.py:32
  218.3 2.4 collective-permute-start
  220.7 6.8 %collective-permute-done = bf16[64,40,768]{2,1,0:T(8,128)(2,1)} collective-permute-done((bf16[64,40,768]{2,1,0:T(8,128)(2,1)}, bf16[64,40,768]{2,1,0:T(8,128)(2,1)}, u32[]{:S(2)}, u32[]{:S(2)}) %collective-permute-start) | collective-permute-done | bytes 3932192 | tf_op jit(solution)/shard_map/ppermute | solution.py:106
  227.4 2.0 broadcast_select_fusion.1
  229.5 0.2 copy.61
  229.7 0.1 reshape.58
  229.8 0.1 reshape_squeeze.16
  229.9 0.7 reshape.59
  230.6 1.5 select_bitcast_fusion.3
  232.1 0.4 pad_maximum_fusion.1
  232.4 0.1 copy.60
  232.6 1.2 reshape_reshape.7
  233.8 3.1 %select_bitcast_fusion.1 = (bf16[64,1,32,768]{3,2,1,0:T(8,128)(2,1)S(1)}, bf16[64,1,32,768]{3,2,1,0:T(8,128)(2,1)S(1)}) fusion(pred[]{:T(512)S(6)} %eq.2, bf16[64,40,768]{2,1,0:T(8,128)(2,1)} %collective-permute-done, bf16[64,40,768]{2,1,0:T(8,128)(2,1)} %all_to_all.23), kind=kLoop, calls=%fused_computation.6 | loop fusion | flops 3145728 | bytes 12582913 | tf_op jit(solution)/shard_map/stack | solution.py:111
  236.9 3.3 %pad_maximum_fusion = bf16[64,2,32,768]{3,2,1,0:T(8,128)(2,1)} fusion(bf16[64,1,32,768]{3,2,1,0:T(8,128)(2,1)S(1)} %get-tuple-element.27, bf16[64,1,32,768]{3,2,1,0:T(8,128)(2,1)S(1)} %get-tuple-element.26), kind=kLoop, calls=%fused_computation.4 | loop fusion | flops 3145728 | bytes 12582912 | tf_op jit(solution)/shard_map/stack | solution.py:111
  (22 shorter events, 0.2 us)
Async XLA Ops:
  0.6 2.3 copy-start.8
  112.8 30.4 %all-to-all-start.1 = ((f32[16,40,768]{2,1,0:T(8,128)}), f32[16,40,768]{2,1,0:T(8,128)S(1)}, u32[]{:S(2)}, u32[]{:S(2)}) async-start(f32[16,40,768]{2,1,0:T(8,128)} %broadcast_in_dim.6), calls=%async_computation.1 | async-start | bytes 3932160 | tf_op jit(solution)/shard_map/all_to_all | solution.py:32
  117.4 39.7 %copy-start.9 = (f32[4,96]{1,0:T(4,128)S(1)}, f32[4,96]{1,0:T(4,128)}, u32[]{:S(2)}) copy-start(f32[4,96]{1,0:T(4,128)} %param.21) | copy-start | bytes 4612
  117.4 39.7 %copy-start.10 = (f32[4,96]{1,0:T(4,128)S(1)}, f32[4,96]{1,0:T(4,128)}, u32[]{:S(2)}) copy-start(f32[4,96]{1,0:T(4,128)} %param.22) | copy-start | bytes 4612
  117.4 39.7 %copy-start.11 = (f32[4,96]{1,0:T(4,128)S(1)}, f32[4,96]{1,0:T(4,128)}, u32[]{:S(2)}) copy-start(f32[4,96]{1,0:T(4,128)} %param.23) | copy-start | bytes 4612
  117.5 40.3 %copy-start.5 = (f32[96,768]{1,0:T(8,128)S(1)}, f32[96,768]{1,0:T(8,128)}, u32[]{:S(2)}) copy-start(f32[96,768]{1,0:T(8,128)} %param.18) | copy-start | bytes 884740
  117.5 40.3 %copy-start.6 = (f32[96,768]{1,0:T(8,128)S(1)}, f32[96,768]{1,0:T(8,128)}, u32[]{:S(2)}) copy-start(f32[96,768]{1,0:T(8,128)} %param.19) | copy-start | bytes 884740
  117.5 40.3 %copy-start.7 = (f32[96,768]{1,0:T(8,128)S(1)}, f32[96,768]{1,0:T(8,128)}, u32[]{:S(2)}) copy-start(f32[96,768]{1,0:T(8,128)} %param.20) | copy-start | bytes 884740
  157.8 1.8 copy-start.3
  158.8 0.7 copy-start.4
  158.9 1.6 copy-start.1
  158.9 2.1 copy-start.2
  163.8 1.1 copy-start
  218.3 9.1 %collective-permute-start = (bf16[64,40,768]{2,1,0:T(8,128)(2,1)}, bf16[64,40,768]{2,1,0:T(8,128)(2,1)}, u32[]{:S(2)}, u32[]{:S(2)}) collective-permute-start(bf16[64,40,768]{2,1,0:T(8,128)(2,1)} %all_to_all.23), channel_id=1, source_target_pairs={{0,8},{8,0},{1,9},{9,1},{2,10},{10,2},{3,11},{11,3},{4,12},{12,4},... | collective-permute-start | bytes 11796488 | tf_op jit(solution)/shard_map/ppermute | solution.py:106
where the time goes:
time: 241 us; the launch traced here: 240 us
  blocking collectives  167 us (69%)
  waiting for transfers between devices  32.5 us (13%)
  other arithmetic  21.5 us (9%)
  local copies, waits for them, and re-layouts  10.2 us (4%)
  starting transfers between devices  6.96 us (3%)
    all_to_all x1, blocking collectives, shards(): received = lax.all_to_all(send, ALL, 0, 0, tiled=True)  103 us
    all_to_all x2, blocking collectives, gather_all(): lax.all_to_all(jnp.broadcast_to(piece[None], (count,) + piece.shape), axi...  63.9 us
    all_to_all x1, waiting for transfers between devices, gather_all(): lax.all_to_all(jnp.broadcast_to(piece[None], (count,) + piece.shape), axi...  25.7 us
    another operation x5, other arithmetic, interleave(): return jnp.stack(pair, axis=1).reshape((n_all, hi - lo) + w_piece.shape[1:])  8.22 us
    ppermute x1, waiting for transfers between devices, shards(): w_other = lax.ppermute(w_mine, 'core', [(0, 1), (1, 0)])  6.75 us
  transfers between devices with their start and end apart: 2, of which 2 were waited for; matrix products, arithmetic and copies ran while one was open for 0% of the time, Pallas kernels for 0%

commit v1 on v0

--- a/solution.py
+++ b/solution.py
@@ -78,7 +78,12 @@
     received = lax.all_to_all(send, ALL, 0, 0, tiled=True)
     reduced = jnp.sum(received.astype(jnp.float32), axis=0)
 
-    block = gather_all(reduced, REP)
+    half_block = gather_all(reduced, "rep_hi")
+    half_other = lax.ppermute(half_block, "core", [(0, 1), (1, 0)])
+    block = jnp.stack(
+        [jnp.where(core == 0, half_block, half_other), jnp.where(core == 0, half_other, half_block)],
+        axis=1,
+    ).reshape((n_rep,) + reduced.shape)
     embed_sum = block[:, :e_rows].reshape(n_rep * e_rows, width)
     proj_sum = block[:, e_rows : e_rows + p_rows].reshape(n_rep * p_rows, width)
     norm_sum = block[:, e_rows + p_rows, :n_vals].reshape(norm_rows, block_norm)

time: 241 us -> 234 us (0.971)
  waiting for transfers between devices: 32.5 us -> 8.6 us
  blocking collectives: 167 us -> 184 us
  other arithmetic: 21.5 us -> 24.8 us
  starting transfers between devices: 6.96 us -> 4.01 us
    all_to_all x1 -> x0, waiting for transfers between devices: 25.7 us -> none  [gather_all(): lax.all_to_all(jnp.broadcast_to(piece[None], (count,) + piece.shape), axi...]
    all_to_all x2 -> x3, blocking collectives: 63.9 us -> 81.1 us  [gather_all(): lax.all_to_all(jnp.broadcast_to(piece[None], (count,) + piece.shape), axi...]
    all_to_all x1 -> x0, starting transfers between devices: 4.61 us -> none  [gather_all(): lax.all_to_all(jnp.broadcast_to(piece[None], (count,) + piece.shape), axi...]
    sub x2, other arithmetic: 3.86 us -> 6.98 us  [adamw(): master_new = master - learning_rate * direction]
where the time goes in v1:
time: 234 us
  blocking collectives  184 us (79%)
  other arithmetic  24.8 us (11%)
  local copies, waits for them, and re-layouts  10.1 us (4%)
  waiting for transfers between devices  8.6 us (4%)
  starting transfers between devices  4.01 us (2%)
    all_to_all x1, blocking collectives, shards(): received = lax.all_to_all(send, ALL, 0, 0, tiled=True)  103 us
    all_to_all x3, blocking collectives, gather_all(): lax.all_to_all(jnp.broadcast_to(piece[None], (count,) + piece.shape), axi...  81.1 us
    another operation x5, other arithmetic, interleave(): return jnp.stack(pair, axis=1).reshape((n_all, hi - lo) + w_piece.shape[1:])  8.22 us
    sub x2, other arithmetic, adamw(): master_new = master - learning_rate * direction  6.98 us
    ppermute x1, waiting for transfers between devices, shards(): w_other = lax.ppermute(w_mine, 'core', [(0, 1), (1, 0)])  6.41 us
  transfers between devices with their start and end apart: 2, of which 2 were waited for; matrix products, arithmetic and copies ran while one was open for 0% of the time, Pallas kernels for 0%

profile of v1, /device:TPU:1, one launch (start us, length us, event | category | flops | bytes accessed | tf_op | source)
XLA Modules:
  0.0 233.5 jit_solution(17529940930619452407)
XLA Ops:
  0.6 0.0 copy-start.5
  0.7 2.2 reshape_squeeze.14
  2.9 0.0 copy-done.5
  2.9 0.1 reshape_squeeze.15
  3.0 0.1 reshape.64
  3.1 3.8 %fusion.1 = bf16[128,40,768]{2,1,0:T(8,128)(2,1)S(1)} fusion(bf16[128,1,24]{2,1,0:T(2,128)(2,1)S(1)} %reshape.64, bf16[128,6,768]{2,1,0:T(8,128)(2,1)S(1)} %reshape_squeeze.14, bf16[128,32,768]{2,1,0:T(8,128)(2,1)} %bitcast.46), kind=kLoop, calls=%fused_computation.3 | loop fusion | flops 31457280 | bytes 15341568 | tf_op jit(solution)/shard_map/concatenate | solution.py:76
  6.9 103.4 %all_to_all.21 = bf16[128,40,768]{2,1,0:T(8,128)(2,1)S(1)} all-to-all(bf16[128,40,768]{2,1,0:T(8,128)(2,1)S(1)} %fusion.1), channel_id=1, replica_groups=mesh['rep_hi'=8,'core'=2,'shard'=8] {'shard','rep_hi','core'}, dimensions={0} | all-to-all | bytes 15728640 | tf_op jit(solution)/shard_map/all_to_all | solution.py:78
  110.3 1.1 convert_reduce_fusion
  111.4 0.1 broadcast_in_dim.6
  111.5 18.0 %all_to_all.22 = f32[8,40,768]{2,1,0:T(8,128)S(1)} all-to-all(f32[8,40,768]{2,1,0:T(8,128)S(1)} %broadcast_in_dim.6), channel_id=1, replica_groups=mesh['rep_hi'=8,'core'=2,'shard'=8] {'rep_hi'}, dimensions={0} | all-to-all | bytes 1966080 | tf_op jit(solution)/shard_map/all_to_all | solution.py:32
  129.5 1.6 collective-permute-start
  131.0 2.2 collective-permute-done
  133.2 0.1 select_bitcast_fusion.3
  133.4 1.1 multiply_reduce_fusion
  134.5 0.6 broadcast_in_dim.7
  135.1 10.8 %all_to_all.23 = f32[8,1,1]{2,1,0:T(1,128)S(1)} all-to-all(f32[8,1,1]{2,1,0:T(1,128)S(1)} %broadcast_in_dim.7), channel_id=1, replica_groups=mesh['rep_hi'=8,'core'=2,'shard'=8] {'shard'}, dimensions={0} | all-to-all | bytes 64 | tf_op jit(solution)/shard_map/all_to_all | solution.py:32
  146.0 0.6 reduce_sum.29
  147.3 0.8 slice_multiply_fusion.1
  148.1 0.2 slice_multiply_fusion
  148.3 0.0 copy-start.3
  148.3 1.2 mul.183
  149.5 0.1 mul.200
  149.6 0.0 copy-done.6
  149.6 0.0 copy-done.7
  149.6 1.3 fusion.10
  150.8 0.1 reshape.60
  150.9 2.2 multiply_subtract_fusion.1
  153.1 0.7 copy-done.4
  153.8 0.0 copy-done.3
  153.8 4.8 %multiply_subtract_fusion = (f32[512,768]{1,0:T(8,128)S(1)}, f32[512,768]{1,0:T(8,128)}, f32[512,768]{1,0:T(8,128)}) fusion(f32[512,768]{1,0:T(8,128)S(1)} %copy-done.3, f32[16,32,768]{2,1,0:T(8,128)S(1)} %slice_multiply_fusion, f32[512,768]{1,0:T(8,128)} %param.16, f32[512,768]{1,0:T(8,128)} %param.17), kind=kLoop, calls=%fused_computation.15 | loop fusion | flops 5898240 | bytes 11010048 | tf_op jit(solution)/shard_map/sub | solution.py:26
  158.7 0.1 dynamic-slice_bitcast_fusion
  158.8 0.3 broadcast_in_dim.8
  159.0 0.8 copy-done.2
  159.8 52.2 %all_to_all.24 = bf16[64,40,768]{2,1,0:T(8,128)(2,1)S(1)} all-to-all(bf16[64,40,768]{2,1,0:T(8,128)(2,1)S(1)} %broadcast_in_dim.8), channel_id=1, replica_groups=mesh['rep_hi'=8,'core'=2,'shard'=8] {'shard','rep_hi'}, dimensions={0} | all-to-all | bytes 7864320 | tf_op jit(solution)/shard_map/all_to_all | solution.py:32
  212.0 2.5 %collective-permute-start.1 = (bf16[64,40,768]{2,1,0:T(8,128)(2,1)S(1)}, bf16[64,40,768]{2,1,0:T(8,128)(2,1)S(1)}, u32[]{:S(2)}, u32[]{:S(2)}) collective-permute-start(bf16[64,40,768]{2,1,0:T(8,128)(2,1)S(1)} %all_to_all.24), channel_id=1, source_target_pairs={{0,8},{8,0},{1,9},{9,1},{2,10},{10,2},{3,11},{11,3},{4,12},{12,4},... | collective-permute-start | bytes 11796488 | tf_op jit(solution)/shard_map/ppermute | solution.py:111
  214.5 6.4 %collective-permute-done.1 = bf16[64,40,768]{2,1,0:T(8,128)(2,1)S(1)} collective-permute-done((bf16[64,40,768]{2,1,0:T(8,128)(2,1)S(1)}, bf16[64,40,768]{2,1,0:T(8,128)(2,1)S(1)}, u32[]{:S(2)}, u32[]{:S(2)}) %collective-permute-start.1) | collective-permute-done | bytes 3932192 | tf_op jit(solution)/shard_map/ppermute | solution.py:111
  220.9 0.6 broadcast_select_fusion.1
  221.5 1.3 copy-done.1
  222.9 0.2 copy.67
  223.1 0.1 reshape.62
  223.2 0.1 reshape_squeeze.16
  223.3 0.7 reshape.63
  224.0 1.5 select_bitcast_fusion.5
  225.4 0.4 pad_maximum_fusion.2
  225.8 0.1 copy.66
  225.9 1.2 reshape_reshape.7
  227.2 3.1 %select_bitcast_fusion.1 = (bf16[64,1,32,768]{3,2,1,0:T(8,128)(2,1)S(1)}, bf16[64,1,32,768]{3,2,1,0:T(8,128)(2,1)S(1)}) fusion(pred[]{:T(512)S(6)} %eq.2, bf16[64,40,768]{2,1,0:T(8,128)(2,1)} %copy-done.1, bf16[64,40,768]{2,1,0:T(8,128)(2,1)} %copy-done), kind=kLoop, calls=%fused_computation.6 | loop fusion | flops 3145728 | bytes 12582913 | tf_op jit(solution)/shard_map/stack | solution.py:116
  230.3 3.3 %pad_maximum_fusion = bf16[64,2,32,768]{3,2,1,0:T(8,128)(2,1)} fusion(bf16[64,1,32,768]{3,2,1,0:T(8,128)(2,1)S(1)} %get-tuple-element.27, bf16[64,1,32,768]{3,2,1,0:T(8,128)(2,1)S(1)} %get-tuple-element.26), kind=kLoop, calls=%fused_computation.4 | loop fusion | flops 3145728 | bytes 12582912 | tf_op jit(solution)/shard_map/stack | solution.py:116
  (16 shorter events, 0.1 us)
Async XLA Ops:
  0.6 2.3 copy-start.5
  129.5 3.8 %collective-permute-start = (f32[8,40,768]{2,1,0:T(8,128)S(1)}, f32[8,40,768]{2,1,0:T(8,128)S(1)}, u32[]{:S(2)}, u32[]{:S(2)}) collective-permute-start(f32[8,40,768]{2,1,0:T(8,128)S(1)} %all_to_all.22), channel_id=1, source_target_pairs={{0,8},{8,0},{1,9},{9,1},{2,10},{10,2},{3,11},{11,3},{4,12},{12,4},... | collective-permute-start | bytes 2949128 | tf_op jit(solution)/shard_map/ppermute | solution.py:82
  148.1 1.5 copy-start.6
  148.1 1.5 copy-start.7
  148.3 5.5 %copy-start.3 = (f32[512,768]{1,0:T(8,128)S(1)}, f32[512,768]{1,0:T(8,128)}, u32[]{:S(2)}) copy-start(f32[512,768]{1,0:T(8,128)} %param.15) | copy-start | bytes 4718596
  153.1 0.7 copy-start.4
  158.6 1.1 copy-start.2
  212.0 8.9 %copy-start = (bf16[64,40,768]{2,1,0:T(8,128)(2,1)}, bf16[64,40,768]{2,1,0:T(8,128)(2,1)S(1)}, u32[]{:S(2)}) copy-start(bf16[64,40,768]{2,1,0:T(8,128)(2,1)S(1)} %all_to_all.24) | copy-start | bytes 11796484
  212.0 8.9 %collective-permute-start.1 = (bf16[64,40,768]{2,1,0:T(8,128)(2,1)S(1)}, bf16[64,40,768]{2,1,0:T(8,128)(2,1)S(1)}, u32[]{:S(2)}, u32[]{:S(2)}) collective-permute-start(bf16[64,40,768]{2,1,0:T(8,128)(2,1)S(1)} %all_to_all.24), channel_id=1, source_target_pairs={{0,8},{8,0},{1,9},{9,1},{2,10},{10,2},{3,11},{11,3},{4,12},{12,4},... | collective-permute-start | bytes 11796488 | tf_op jit(solution)/shard_map/ppermute | solution.py:111
  220.9 1.9 copy-start.1
